TPU v7x, 128 devices: a whole 4x4x4 slice. The times are simulated.
128 devices in a mesh: leaf: 16 (over x, y), col: 8 (over z, core).
Axes of the slice: x: 4, y: 4, z: 4, core: 2. Of those that a mesh axis runs over, the one named last changes fastest.
Arguments:
- right_side: float32 [31, 2560, 256], P(None, 'leaf'), may hold values from -6 to 6
- reciprocal_pivot_matrix: bfloat16 [31, 2560, 2560], P(None, 'col', 'leaf'), as said below
- panels: bfloat16 [98, 2560, 2560], P(None, 'leaf', 'col'), may hold values from -0.03125 to 0.03125
- parent: int32 [31], replicated, may hold values from 16 to 30, as said below
Outputs:
- solution: float32 [31, 2560, 256], P(None, 'leaf')
Inputs may be any that keep to these rules, and one draw needn't show every extreme that they name: Supernodes 0 to 15 have parents among 16 to 23, 16 to 23 among 24 to 27, 24 to 27 among 28 and 29, 28 and 29 have parent 30, and entry 30 is 30 itself; each supernode of levels 1 to 4 is the parent of exactly two supernodes of the level below. `reciprocal_pivot_matrix`: each block is lower triangular with a positive diagonal.
All inputs are finite; a program needn't handle non-finite values.
Results may differ from a plain program's by a relative error of at most 0.03.
Values may be sent and summed in bfloat16 or wider, within the bound.
No kernel may reach another device: no remote copies, remote signals or barrier semaphores. Data moves between devices by JAX's collectives and lax.ppermute only.
A program may use at most 192 MiB of HBM per device.

v0:
```python
import jax
import jax.numpy as jnp
import numpy as np
from jax import lax
from jax.sharding import PartitionSpec as P

level_starts = (0, 16, 24, 28, 30)
level_counts = (16, 8, 4, 2, 1)


def pair_table():
    sources = []
    distances = []
    for tree_level in range(5):
        for tree_vertex in range(
            level_starts[tree_level], level_starts[tree_level] + level_counts[tree_level]
        ):
            for distance in range(1, 5 - tree_level):
                sources.append(tree_vertex)
                distances.append(distance)
    return (sources, distances)


def node_level(tree_vertex):
    deepest = 0
    for tree_level in range(5):
        if level_starts[tree_level] <= tree_vertex:
            deepest = tree_level
    return deepest


def pair_offset(tree_level):
    initial_position = 0
    for lower in range(tree_level):
        initial_position = initial_position + level_counts[lower] * (4 - lower)
    return initial_position


def pair_ancestors(parent):
    sources, distances = pair_table()
    climbed = [jnp.arange(parent.shape[0], dtype=jnp.int32)]
    for distance in range(4):
        climbed.append(parent[climbed[-1]])
    return jnp.stack(
        [climbed[distance][source_node] for source_node, distance in zip(sources, distances)]
    )


def forward_products(panel_local, forward_stack, ancestor, pair_list, start_node, node_count):
    sources, distances = pair_table()
    chosen = np.array(pair_list, dtype=np.int32)
    feeders = np.array([sources[node_pairing] for node_pairing in pair_list], dtype=np.int32)
    products = jnp.einsum(
        "sjv,svk->sjk",
        panel_local[chosen],
        forward_stack[feeders],
        preferred_element_type=jnp.float32,
    )
    slots = jnp.arange(node_count, dtype=jnp.int32) + start_node
    onehot = (slots[:, None] == ancestor[chosen][None, :]).astype(jnp.float32)
    return jnp.einsum("kp,par->kar", onehot, products, precision=lax.Precision.HIGHEST)


def solve(right_side, diag_local, panel_local, ancestor):
    sources, distances = pair_table()
    node_total = right_side.shape[0]
    load_vector_count = right_side.shape[2]
    col_rows = diag_local.shape[1]
    leaf_rows = diag_local.shape[2]
    forward_stack = jnp.zeros((node_total, col_rows, load_vector_count), jnp.bfloat16)
    forward_levels = [None] * 5
    for tree_level in range(5):
        start_node = level_starts[tree_level]
        node_count = level_counts[tree_level]
        reduced = right_side[start_node : start_node + node_count]
        if tree_level > 0:
            arriving = [
                node_pairing
                for node_pairing in range(len(sources))
                if node_level(sources[node_pairing]) + distances[node_pairing] == tree_level
            ]
            partial_value = forward_products(
                panel_local, forward_stack, ancestor, arriving, start_node, node_count
            )
            reduced = reduced - lax.psum(partial_value.astype(jnp.bfloat16), "col").astype(
                jnp.float32
            )
        division_count = jnp.einsum(
            "kcl,klr->kcr",
            diag_local[start_node : start_node + node_count],
            reduced.astype(jnp.bfloat16),
            preferred_element_type=jnp.float32,
        )
        forward_value = lax.psum(division_count.astype(jnp.bfloat16), "leaf").astype(jnp.float32)
        forward_levels[tree_level] = forward_value
        forward_stack = forward_stack.at[start_node : start_node + node_count].set(
            forward_value.astype(jnp.bfloat16)
        )
    solution_stack = jnp.zeros((node_total, leaf_rows, load_vector_count), jnp.bfloat16)
    results = [None] * 5
    for tree_level in (4, 3, 2, 1, 0):
        start_node = level_starts[tree_level]
        node_count = level_counts[tree_level]
        corrected = forward_levels[tree_level]
        if tree_level < 4:
            initial_position = pair_offset(tree_level)
            span_pairs = node_count * (4 - tree_level)
            upper_node = solution_stack[ancestor[initial_position : initial_position + span_pairs]]
            products = jnp.einsum(
                "boj,boh->bjh",
                panel_local[initial_position : initial_position + span_pairs],
                upper_node,
                preferred_element_type=jnp.float32,
            )
            partial_value = jnp.sum(
                products.reshape(node_count, 4 - tree_level, col_rows, load_vector_count), axis=1
            )
            corrected = corrected - lax.psum(partial_value.astype(jnp.bfloat16), "leaf").astype(
                jnp.float32
            )
        division_count = jnp.einsum(
            "kcl,kcr->klr",
            diag_local[start_node : start_node + node_count],
            corrected.astype(jnp.bfloat16),
            preferred_element_type=jnp.float32,
        )
        solution = lax.psum(division_count.astype(jnp.bfloat16), "col").astype(jnp.float32)
        results[tree_level] = solution
        solution_stack = solution_stack.at[start_node : start_node + node_count].set(
            solution.astype(jnp.bfloat16)
        )
    return jnp.concatenate(results, axis=0)


def shards(right_side, reciprocal_pivot_matrix, panels, parent):
    ancestor = pair_ancestors(parent)
    return solve(right_side, reciprocal_pivot_matrix, panels, ancestor)


def solution(mesh):
    return jax.shard_map(
        shards,
        mesh=mesh,
        in_specs=(P(None, "leaf", None), P(None, "col", "leaf"), P(None, "leaf", "col"), P()),
        out_specs=P(None, "leaf", None),
        check_vma=False,
    )
```

profile of v0, /device:TPU:0, one launch (start us, length us, event | category | flops | bytes accessed | tf_op | source)
XLA Modules:
  0.0 1465.1 jit_solution(12247454413178244909)
XLA Ops:
  18.7 62.5 %stack.204 = s32[98]{0:T(128)S(1)} concatenate(s32[1]{0:T(128)} %get-tuple-element.201, s32[1]{0:T(128)} %get-tuple-element.184, s32[1]{0:T(128)} %get-tuple-element.198, s32[1]{0:T(128)} %get-tuple-element.175, s32[1]{0:T(128)} %get-tuple-element.202, s32[1]{0:T(128)} %get-tuple-element.183, s32[1]{0:T(128)} %get-tuple-element.197, s32[1]{0:T(128)} %get-tuple-element.174, ...), dimensions={0} | concatenate | bytes 784 | tf_op jit(solution)/shard_map/stack | solution.py:44
  87.3 19.3 %all-reduce.21.cloned.1.call-done = bf16[16,320,256]{2,1,0:T(8,128)(2,1)} async-done(((bf16[16,320,256]{2,1,0:T(8,128)(2,1)}), bf16[16,320,256]{2,1,0:T(8,128)(2,1)}) %all-reduce.21.cloned.1.call-update) | async-done | bytes 2621456 | tf_op jit(solution)/shard_map/psum | solution.py:94
  122.0 61.0 %all-reduce.23.cloned.1.call-done = bf16[8,160,256]{2,1,0:T(8,128)(2,1)} async-done(((bf16[8,160,256]{2,1,0:T(8,128)(2,1)}), bf16[8,160,256]{2,1,0:T(8,128)(2,1)}) %all-reduce.23.cloned.1.call-update) | async-done | bytes 655376 | tf_op jit(solution)/shard_map/psum | solution.py:85
  186.9 7.2 gather_fusion.10
  194.8 78.5 %all-reduce.25.cloned.1.call-done = bf16[8,320,256]{2,1,0:T(8,128)(2,1)} async-done(((bf16[8,320,256]{2,1,0:T(8,128)(2,1)}), bf16[8,320,256]{2,1,0:T(8,128)(2,1)}) %all-reduce.25.cloned.1.call-update) | async-done | bytes 1310736 | tf_op jit(solution)/shard_map/psum | solution.py:94
  289.7 59.9 %all-reduce.27.cloned.1.call-done = bf16[4,160,256]{2,1,0:T(8,128)(2,1)} async-done(((bf16[4,160,256]{2,1,0:T(8,128)(2,1)}), bf16[4,160,256]{2,1,0:T(8,128)(2,1)}) %all-reduce.27.cloned.1.call-update) | async-done | bytes 327696 | tf_op jit(solution)/shard_map/psum | solution.py:85
  352.8 7.3 gather_fusion.13
  360.8 76.0 %all-reduce.29.cloned.1.call-done = bf16[4,320,256]{2,1,0:T(8,128)(2,1)} async-done(((bf16[4,320,256]{2,1,0:T(8,128)(2,1)}), bf16[4,320,256]{2,1,0:T(8,128)(2,1)}) %all-reduce.29.cloned.1.call-update) | async-done | bytes 655376 | tf_op jit(solution)/shard_map/psum | solution.py:94
  454.0 57.4 %all-reduce.31.cloned.1.call-done = bf16[2,160,256]{2,1,0:T(8,128)(2,1)} async-done(((bf16[2,160,256]{2,1,0:T(8,128)(2,1)}), bf16[2,160,256]{2,1,0:T(8,128)(2,1)}) %all-reduce.31.cloned.1.call-update) | async-done | bytes 163856 | tf_op jit(solution)/shard_map/psum | solution.py:85
  513.8 7.4 gather_fusion.5
  522.0 76.1 %all-reduce.33.cloned.1.call-done = bf16[2,320,256]{2,1,0:T(8,128)(2,1)} async-done(((bf16[2,320,256]{2,1,0:T(8,128)(2,1)}), bf16[2,320,256]{2,1,0:T(8,128)(2,1)}) %all-reduce.33.cloned.1.call-update) | async-done | bytes 327696 | tf_op jit(solution)/shard_map/psum | solution.py:94
  615.7 54.3 %all-reduce.35.cloned.1.call-done = bf16[1,160,256]{2,1,0:T(8,128)(2,1)} async-done(((bf16[1,160,256]{2,1,0:T(8,128)(2,1)}), bf16[1,160,256]{2,1,0:T(8,128)(2,1)}) %all-reduce.35.cloned.1.call-update) | async-done | bytes 81936 | tf_op jit(solution)/shard_map/psum | solution.py:85
  672.0 84.8 %all-reduce.37.cloned.1.call-done = bf16[320,256]{0,1:T(8,128)(2,1)} async-done(((bf16[320,256]{0,1:T(8,128)(2,1)}), bf16[320,256]{0,1:T(8,128)(2,1)}) %all-reduce.37.cloned.1.call-update) | async-done | bytes 163856 | tf_op jit(solution)/shard_map/psum | solution.py:94
  758.7 54.4 %all-reduce.39.cloned.1.call-done = bf16[1,160,256]{2,1,0:T(8,128)(2,1)} async-done(((bf16[1,160,256]{2,1,0:T(8,128)(2,1)}), bf16[1,160,256]{2,1,0:T(8,128)(2,1)}) %all-reduce.39.cloned.1.call-update) | async-done | bytes 81936 | tf_op jit(solution)/shard_map/psum | solution.py:127
  822.9 78.6 %all-reduce.41.cloned.1.call-done = bf16[2,320,256]{2,1,0:T(8,128)(2,1)} async-done(((bf16[2,320,256]{2,1,0:T(8,128)(2,1)}), bf16[2,320,256]{2,1,0:T(8,128)(2,1)}) %all-reduce.41.cloned.1.call-update) | async-done | bytes 327696 | tf_op jit(solution)/shard_map/psum | solution.py:118
  903.6 57.6 %all-reduce.43.cloned.1.call-done = bf16[2,160,256]{2,1,0:T(8,128)(2,1)} async-done(((bf16[2,160,256]{2,1,0:T(8,128)(2,1)}), bf16[2,160,256]{2,1,0:T(8,128)(2,1)}) %all-reduce.43.cloned.1.call-update) | async-done | bytes 163856 | tf_op jit(solution)/shard_map/psum | solution.py:127
  966.7 15.4 %stack.238 = s32[24,1]{0,1:T(1,128)S(1)} concatenate(s32[1,1]{0,1:T(1,128)} %bitcast.34, s32[1,1]{0,1:T(1,128)} %bitcast.35, s32[1,1]{0,1:T(1,128)} %bitcast.36, s32[1,1]{0,1:T(1,128)} %bitcast.37, s32[1,1]{0,1:T(1,128)} %bitcast.38, s32[1,1]{0,1:T(1,128)} %bitcast.39, s32[1,1]{0,1:T(1,128)} %bitcast.40, s32[1,1]{0,1:T(1,128)} %bitcast.41, s32[1,1]{0,1:T(1,128)} %bitcast.42, ...), dimensions={0} | concatenate | bytes 192 | tf_op jit(solution)/shard_map/stack | solution.py:44
  982.1 69.6 %all-reduce.45.cloned.1.call-done = bf16[4,320,256]{2,1,0:T(8,128)(2,1)} async-done(((bf16[4,320,256]{2,1,0:T(8,128)(2,1)}), bf16[4,320,256]{2,1,0:T(8,128)(2,1)}) %all-reduce.45.cloned.1.call-update) | async-done | bytes 655376 | tf_op jit(solution)/shard_map/psum | solution.py:118
  1054.3 59.6 %all-reduce.47.cloned.1.call-done = bf16[4,160,256]{2,1,0:T(8,128)(2,1)} async-done(((bf16[4,160,256]{2,1,0:T(8,128)(2,1)}), bf16[4,160,256]{2,1,0:T(8,128)(2,1)}) %all-reduce.47.cloned.1.call-update) | async-done | bytes 327696 | tf_op jit(solution)/shard_map/psum | solution.py:127
  1130.3 85.5 %all-reduce.49.cloned.1.call-done = bf16[8,320,256]{2,1,0:T(8,128)(2,1)} async-done(((bf16[8,320,256]{2,1,0:T(8,128)(2,1)}), bf16[8,320,256]{2,1,0:T(8,128)(2,1)}) %all-reduce.49.cloned.1.call-update) | async-done | bytes 1310736 | tf_op jit(solution)/shard_map/psum | solution.py:118
  1219.3 61.0 %all-reduce.51.cloned.1.call-done = bf16[8,160,256]{2,1,0:T(8,128)(2,1)} async-done(((bf16[8,160,256]{2,1,0:T(8,128)(2,1)}), bf16[8,160,256]{2,1,0:T(8,128)(2,1)}) %all-reduce.51.cloned.1.call-update) | async-done | bytes 655376 | tf_op jit(solution)/shard_map/psum | solution.py:127
  1284.7 8.7 bitcast_reduce_fusion
  1293.5 91.8 %all-reduce.53.cloned.1.call-done = bf16[16,320,256]{2,1,0:T(8,128)(2,1)} async-done(((bf16[16,320,256]{2,1,0:T(8,128)(2,1)}), bf16[16,320,256]{2,1,0:T(8,128)(2,1)}) %all-reduce.53.cloned.1.call-update) | async-done | bytes 2621456 | tf_op jit(solution)/shard_map/psum | solution.py:118
  1390.4 63.1 %all-reduce.55.cloned.1.call-done = bf16[16,160,256]{2,1,0:T(8,128)(2,1)} async-done(((bf16[16,160,256]{2,1,0:T(8,128)(2,1)}), bf16[16,160,256]{2,1,0:T(8,128)(2,1)}) %all-reduce.55.cloned.1.call-update) | async-done | bytes 1310736 | tf_op jit(solution)/shard_map/psum | solution.py:127
  (154 shorter events, 153.7 us)
Async XLA Ops:
  6.5 100.1 %all-reduce.21.cloned.1.call-start = ((), (), s32[]{:S(2)}) async-start(), calls=%async_computation | async-start | bytes 5242880 | tf_op jit(solution)/shard_map/psum | solution.py:94
  11.4 171.6 %all-reduce.23.cloned.1.call-start = ((), (), s32[]{:S(2)}) async-start(), calls=%async_computation.1 | async-start | bytes 1310720 | tf_op jit(solution)/shard_map/psum | solution.py:85
  120.9 66.0 %copy-start.10 = (s32[24]{0:T(128)S(1)}, s32[24]{0:T(128)}, u32[]{:S(2)}) copy-start(s32[24]{0:T(128)} %constant.265) | copy-start | bytes 292
  122.0 151.3 %all-reduce.25.cloned.1.call-start = ((), (), s32[]{:S(2)}) async-start(), calls=%async_computation.2 | async-start | bytes 2621440 | tf_op jit(solution)/shard_map/psum | solution.py:94
  186.6 163.1 %all-reduce.27.cloned.1.call-start = ((), (), s32[]{:S(2)}) async-start(), calls=%async_computation.3 | async-start | bytes 655360 | tf_op jit(solution)/shard_map/psum | solution.py:85
  285.2 67.6 %copy-start.9 = (s32[28]{0:T(128)S(1)}, s32[28]{0:T(128)}, u32[]{:S(2)}) copy-start(s32[28]{0:T(128)} %constant.267) | copy-start | bytes 340
  289.6 147.2 %all-reduce.29.cloned.1.call-start = ((), (), s32[]{:S(2)}) async-start(), calls=%async_computation.4 | async-start | bytes 1310720 | tf_op jit(solution)/shard_map/psum | solution.py:94
  352.2 159.2 %all-reduce.31.cloned.1.call-start = ((), (), s32[]{:S(2)}) async-start(), calls=%async_computation.5 | async-start | bytes 327680 | tf_op jit(solution)/shard_map/psum | solution.py:85
  448.9 64.9 %copy-start.8 = (s32[30]{0:T(128)S(1)}, s32[30]{0:T(128)}, u32[]{:S(2)}) copy-start(s32[30]{0:T(128)} %constant.263) | copy-start | bytes 364
  454.0 144.1 %all-reduce.33.cloned.1.call-start = ((), (), s32[]{:S(2)}) async-start(), calls=%async_computation.6 | async-start | bytes 655360 | tf_op jit(solution)/shard_map/psum | solution.py:94
  513.6 156.4 %all-reduce.35.cloned.1.call-start = ((), (), s32[]{:S(2)}) async-start(), calls=%async_computation.7 | async-start | bytes 163840 | tf_op jit(solution)/shard_map/psum | solution.py:85
  614.9 286.5 %copy-start.5 = (bf16[2,320,256]{2,1,0:T(8,128)(2,1)S(1)}, bf16[2,320,256]{2,1,0:T(8,128)(2,1)}, u32[]{:S(2)}) copy-start(bf16[2,320,256]{2,1,0:T(8,128)(2,1)} %all-reduce.33.cloned.1.call-done) | copy-start | bytes 983044
  615.6 141.1 %all-reduce.37.cloned.1.call-start = ((), (), s32[]{:S(2)}) async-start(), calls=%async_computation.8 | async-start | bytes 393216 | tf_op jit(solution)/shard_map/psum | solution.py:94
  671.9 141.1 %all-reduce.39.cloned.1.call-start = ((), (), s32[]{:S(2)}) async-start(), calls=%async_computation.9 | async-start | bytes 163840 | tf_op jit(solution)/shard_map/psum | solution.py:127
  758.6 142.8 %all-reduce.41.cloned.1.call-start = ((), (), s32[]{:S(2)}) async-start(), calls=%async_computation.10 | async-start | bytes 655360 | tf_op jit(solution)/shard_map/psum | solution.py:118
  815.4 236.2 %copy-start.2 = (bf16[4,320,256]{2,1,0:T(8,128)(2,1)S(1)}, bf16[4,320,256]{2,1,0:T(8,128)(2,1)}, u32[]{:S(2)}) copy-start(bf16[4,320,256]{2,1,0:T(8,128)(2,1)} %all-reduce.29.cloned.1.call-done) | copy-start | bytes 1966084
  817.6 143.6 %all-reduce.43.cloned.1.call-start = ((), (), s32[]{:S(2)}) async-start(), calls=%async_computation.11 | async-start | bytes 327680 | tf_op jit(solution)/shard_map/psum | solution.py:127
  903.5 148.2 %all-reduce.45.cloned.1.call-start = ((), (), s32[]{:S(2)}) async-start(), calls=%async_computation.12 | async-start | bytes 1310720 | tf_op jit(solution)/shard_map/psum | solution.py:118
  966.6 147.3 %all-reduce.47.cloned.1.call-start = ((), (), s32[]{:S(2)}) async-start(), calls=%async_computation.13 | async-start | bytes 655360 | tf_op jit(solution)/shard_map/psum | solution.py:127
  1054.1 161.8 %all-reduce.49.cloned.1.call-start = ((), (), s32[]{:S(2)}) async-start(), calls=%async_computation.14 | async-start | bytes 2621440 | tf_op jit(solution)/shard_map/psum | solution.py:118
  1129.2 151.2 %all-reduce.51.cloned.1.call-start = ((), (), s32[]{:S(2)}) async-start(), calls=%async_computation.15 | async-start | bytes 1310720 | tf_op jit(solution)/shard_map/psum | solution.py:127
  1219.2 166.1 %all-reduce.53.cloned.1.call-start = ((), (), s32[]{:S(2)}) async-start(), calls=%async_computation.16 | async-start | bytes 5242880 | tf_op jit(solution)/shard_map/psum | solution.py:118
  1293.4 160.1 %all-reduce.55.cloned.1.call-start = ((), (), s32[]{:S(2)}) async-start(), calls=%async_computation.17 | async-start | bytes 2621440 | tf_op jit(solution)/shard_map/psum | solution.py:127
  1390.4 64.6 %copy-start.7 = (bf16[1,160,256]{2,1,0:T(8,128)(2,1)S(1)}, bf16[1,160,256]{2,1,0:T(8,128)(2,1)}, u32[]{:S(2)}) copy-start(bf16[1,160,256]{2,1,0:T(8,128)(2,1)} %all-reduce.39.cloned.1.call-done) | copy-start | bytes 245764
  (5 other events, 201.6 us)
Sparse Core Ops, SparseCore 0:
  11.5 95.1 all-reduce.20
  122.1 60.9 all-reduce.22
  186.7 86.5 all-reduce.24
  289.7 59.8 all-reduce.26
  352.7 84.0 all-reduce.28
  454.1 57.2 all-reduce.30
  514.9 83.1 all-reduce.32
  615.7 54.1 all-reduce.34
  673.1 83.5 all-reduce.36
  758.9 54.0 all-reduce.38
  817.7 83.6 all-reduce.40
  903.7 57.3 all-reduce.42
  966.7 84.9 all-reduce.44
  1054.2 59.7 all-reduce.46
  1129.3 86.4 all-reduce.48
  1219.4 60.9 all-reduce.50
  1293.5 91.7 all-reduce.52
  1390.5 62.9 all-reduce.54
where the time goes:
time: 1470 us
  waiting for transfers between devices  1190 us (81%)
  local copies, waits for them, and re-layouts  170 us (12%)
  matrix products  82 us (6%)
    psum x5, waiting for transfers between devices, solve(): lax.psum(division_count.astype(jnp.bfloat16), 'leaf').astype(jnp.float32)  335 us
    psum x4, waiting for transfers between devices, solve(): lax.psum(partial_value.astype(jnp.bfloat16), 'leaf').astype(jnp.float32)  326 us
    psum x5, waiting for transfers between devices, solve(): lax.psum(division_count.astype(jnp.bfloat16), 'col').astype(jnp.float32)  296 us
    psum x4, waiting for transfers between devices, solve(): lax.psum(partial_value.astype(jnp.bfloat16), 'col').astype(jnp.float32)  233 us
    another operation x4, local copies, waits for them, and re-layouts, pair_ancestors(): jnp.stack([climbed[distance][source_node] for source_node, distance in zi...  84.2 us
  transfers between devices with their start and end apart: 18, of which 18 were waited for; matrix products, arithmetic and copies ran while one was open for 8% of the time, Pallas kernels for 0%

commit v1 on v0

--- a/solution.py
+++ b/solution.py
@@ -91,7 +91,12 @@
             reduced.astype(jnp.bfloat16),
             preferred_element_type=jnp.float32,
         )
-        forward_value = lax.psum(division_count.astype(jnp.bfloat16), "leaf").astype(jnp.float32)
+
+        def mark_matrix(target):
+            new = jax.lax.all_gather(target, "leaf").sum(axis=0)
+            return new
+
+        forward_value = mark_matrix(division_count.astype(jnp.bfloat16)).astype(jnp.float32)
         forward_levels[tree_level] = forward_value
         forward_stack = forward_stack.at[start_node : start_node + node_count].set(
             forward_value.astype(jnp.bfloat16)

time: 1470 us -> 1630 us (1.11)
  waiting for transfers between devices: 1190 us -> 1310 us
  other arithmetic: 8.48 us -> 50.6 us
    all_gather x0 -> x5, waiting for transfers between devices: none -> 453 us  [mark_matrix(): new = jax.lax.all_gather(target, 'leaf').sum(axis=0)]
    psum x5 -> x0, waiting for transfers between devices: 335 us -> none  [solve(): lax.psum(division_count.astype(jnp.bfloat16), 'leaf').astype(jnp.float32)]
    reduce_sum x0 -> x5, other arithmetic: none -> 38.9 us  [mark_matrix(): new = jax.lax.all_gather(target, 'leaf').sum(axis=0)]
where the time goes in v1:
time: 1630 us; the launch traced here: 1620 us
  waiting for transfers between devices  1310 us (80%)
  local copies, waits for them, and re-layouts  167 us (10%)
  matrix products  82.6 us (5%)
  other arithmetic  50.6 us (3%)
    all_gather x5, waiting for transfers between devices, mark_matrix(): new = jax.lax.all_gather(target, 'leaf').sum(axis=0)  453 us
    psum x4, waiting for transfers between devices, solve(): lax.psum(partial_value.astype(jnp.bfloat16), 'leaf').astype(jnp.float32)  326 us
    psum x5, waiting for transfers between devices, solve(): lax.psum(division_count.astype(jnp.bfloat16), 'col').astype(jnp.float32)  295 us
    psum x4, waiting for transfers between devices, solve(): lax.psum(partial_value.astype(jnp.bfloat16), 'col').astype(jnp.float32)  234 us
    another operation x4, local copies, waits for them, and re-layouts, pair_ancestors(): jnp.stack([climbed[distance][source_node] for source_node, distance in zi...  82.7 us
    reduce_sum x5, other arithmetic, mark_matrix(): new = jax.lax.all_gather(target, 'leaf').sum(axis=0)  38.9 us
  transfers between devices with their start and end apart: 18, of which 18 were waited for; matrix products, arithmetic and copies ran while one was open for 8% of the time, Pallas kernels for 0%

profile of v1, /device:TPU:0, one launch (start us, length us, event | category | flops | bytes accessed | tf_op | source)
XLA Modules:
  0.0 1624.9 jit_solution(7201858033078469960)
XLA Ops:
  18.7 61.5 %stack.204 = s32[98]{0:T(128)S(1)} concatenate(s32[1]{0:T(128)} %get-tuple-element.207, s32[1]{0:T(128)} %get-tuple-element.184, s32[1]{0:T(128)} %get-tuple-element.198, s32[1]{0:T(128)} %get-tuple-element.175, s32[1]{0:T(128)} %get-tuple-element.208, s32[1]{0:T(128)} %get-tuple-element.183, s32[1]{0:T(128)} %get-tuple-element.197, s32[1]{0:T(128)} %get-tuple-element.174, ...), dimensions={0} | concatenate | bytes 784 | tf_op jit(solution)/shard_map/stack | solution.py:44
  80.9 8.7 gather_fusion.7
  89.6 164.2 %all-gather.11.cloned.1.call-done = bf16[256,320,256]{2,1,0:T(8,128)(2,1)} async-done(((bf16[16,320,256]{2,1,0:T(8,128)(2,1)}), bf16[256,320,256]{2,1,0:T(8,128)(2,1)}) %all-gather.11.cloned.1.call-update) | async-done | bytes 41943056 | tf_op jit(solution)/shard_map/all_gather | solution.py:96
  253.8 15.8 reduce_sum.91
  285.0 61.4 %all-reduce.16.cloned.1.call-done = bf16[8,160,256]{2,0,1:T(8,128)(2,1)} async-done(((bf16[8,160,256]{2,0,1:T(8,128)(2,1)}), bf16[8,160,256]{2,0,1:T(8,128)(2,1)}) %all-reduce.16.cloned.1.call-update) | async-done | bytes 655376 | tf_op jit(solution)/shard_map/psum | solution.py:85
  359.3 123.7 %all-gather.13.cloned.1.call-done = bf16[128,320,256]{2,1,0:T(8,128)(2,1)} async-done(((bf16[8,320,256]{2,1,0:T(8,128)(2,1)}), bf16[128,320,256]{2,1,0:T(8,128)(2,1)}) %all-gather.13.cloned.1.call-update) | async-done | bytes 20971536 | tf_op jit(solution)/shard_map/all_gather | solution.py:96
  483.0 11.6 reduce_sum.92
  509.6 60.3 %all-reduce.18.cloned.1.call-done = bf16[4,160,256]{2,0,1:T(4,128)(2,1)} async-done(((bf16[4,160,256]{2,0,1:T(4,128)(2,1)}), bf16[4,160,256]{2,0,1:T(4,128)(2,1)}) %all-reduce.18.cloned.1.call-update) | async-done | bytes 327696 | tf_op jit(solution)/shard_map/psum | solution.py:85
  582.2 71.0 %all-gather.15.cloned.1.call-done = bf16[64,320,256]{2,1,0:T(8,128)(2,1)} async-done(((bf16[4,320,256]{2,1,0:T(8,128)(2,1)}), bf16[64,320,256]{2,1,0:T(8,128)(2,1)}) %all-gather.15.cloned.1.call-update) | async-done | bytes 10485776 | tf_op jit(solution)/shard_map/all_gather | solution.py:96
  675.4 57.8 %all-reduce.20.cloned.1.call-done = bf16[2,160,256]{2,1,0:T(8,128)(2,1)} async-done(((bf16[2,160,256]{2,1,0:T(8,128)(2,1)}), bf16[2,160,256]{2,1,0:T(8,128)(2,1)}) %all-reduce.20.cloned.1.call-update) | async-done | bytes 163856 | tf_op jit(solution)/shard_map/psum | solution.py:85
  744.0 47.6 %all-gather.17.cloned.1.call-done = bf16[32,320,256]{2,1,0:T(8,128)(2,1)} async-done(((bf16[2,320,256]{2,1,0:T(8,128)(2,1)}), bf16[32,320,256]{2,1,0:T(8,128)(2,1)}) %all-gather.17.cloned.1.call-update) | async-done | bytes 5242896 | tf_op jit(solution)/shard_map/all_gather | solution.py:96
  811.5 54.6 %all-reduce.22.cloned.1.call-done = bf16[1,160,256]{2,1,0:T(8,128)(2,1)} async-done(((bf16[1,160,256]{2,1,0:T(8,128)(2,1)}), bf16[1,160,256]{2,1,0:T(8,128)(2,1)}) %all-reduce.22.cloned.1.call-update) | async-done | bytes 81936 | tf_op jit(solution)/shard_map/psum | solution.py:85
  868.1 47.0 %all-gather.19.cloned.1.call-done = bf16[5120,256]{1,0:T(8,128)(2,1)} async-done(((bf16[320,256]{1,0:T(8,128)(2,1)}), bf16[5120,256]{1,0:T(8,128)(2,1)}) %all-gather.19.cloned.1.call-update) | async-done | bytes 2621456 | tf_op jit(solution)/shard_map/all_gather | solution.py:96
  919.0 54.1 %all-reduce.24.cloned.1.call-done = bf16[1,160,256]{2,1,0:T(8,128)(2,1)} async-done(((bf16[1,160,256]{2,1,0:T(8,128)(2,1)}), bf16[1,160,256]{2,1,0:T(8,128)(2,1)}) %all-reduce.24.cloned.1.call-update) | async-done | bytes 81936 | tf_op jit(solution)/shard_map/psum | solution.py:132
  982.8 78.6 %all-reduce.26.cloned.1.call-done = bf16[2,320,256]{2,1,0:T(8,128)(2,1)} async-done(((bf16[2,320,256]{2,1,0:T(8,128)(2,1)}), bf16[2,320,256]{2,1,0:T(8,128)(2,1)}) %all-reduce.26.cloned.1.call-update) | async-done | bytes 327696 | tf_op jit(solution)/shard_map/psum | solution.py:123
  1063.6 57.5 %all-reduce.28.cloned.1.call-done = bf16[2,160,256]{2,1,0:T(8,128)(2,1)} async-done(((bf16[2,160,256]{2,1,0:T(8,128)(2,1)}), bf16[2,160,256]{2,1,0:T(8,128)(2,1)}) %all-reduce.28.cloned.1.call-update) | async-done | bytes 163856 | tf_op jit(solution)/shard_map/psum | solution.py:132
  1126.5 15.0 stack.238
  1141.5 70.1 %all-reduce.30.cloned.1.call-done = bf16[4,320,256]{2,1,0:T(8,128)(2,1)} async-done(((bf16[4,320,256]{2,1,0:T(8,128)(2,1)}), bf16[4,320,256]{2,1,0:T(8,128)(2,1)}) %all-reduce.30.cloned.1.call-update) | async-done | bytes 655376 | tf_op jit(solution)/shard_map/psum | solution.py:123
  1214.2 59.6 %all-reduce.32.cloned.1.call-done = bf16[4,160,256]{2,1,0:T(8,128)(2,1)} async-done(((bf16[4,160,256]{2,1,0:T(8,128)(2,1)}), bf16[4,160,256]{2,1,0:T(8,128)(2,1)}) %all-reduce.32.cloned.1.call-update) | async-done | bytes 327696 | tf_op jit(solution)/shard_map/psum | solution.py:132
  1290.2 85.5 %all-reduce.34.cloned.1.call-done = bf16[8,320,256]{2,1,0:T(8,128)(2,1)} async-done(((bf16[8,320,256]{2,1,0:T(8,128)(2,1)}), bf16[8,320,256]{2,1,0:T(8,128)(2,1)}) %all-reduce.34.cloned.1.call-update) | async-done | bytes 1310736 | tf_op jit(solution)/shard_map/psum | solution.py:123
  1379.2 61.0 %all-reduce.36.cloned.1.call-done = bf16[8,160,256]{2,1,0:T(8,128)(2,1)} async-done(((bf16[8,160,256]{2,1,0:T(8,128)(2,1)}), bf16[8,160,256]{2,1,0:T(8,128)(2,1)}) %all-reduce.36.cloned.1.call-update) | async-done | bytes 655376 | tf_op jit(solution)/shard_map/psum | solution.py:132
  1444.5 8.7 bitcast_reduce_fusion
  1453.3 91.9 %all-reduce.38.cloned.1.call-done = bf16[16,320,256]{2,1,0:T(8,128)(2,1)} async-done(((bf16[16,320,256]{2,1,0:T(8,128)(2,1)}), bf16[16,320,256]{2,1,0:T(8,128)(2,1)}) %all-reduce.38.cloned.1.call-update) | async-done | bytes 2621456 | tf_op jit(solution)/shard_map/psum | solution.py:123
  1550.3 63.1 %all-reduce.40.cloned.1.call-done = bf16[16,160,256]{2,1,0:T(8,128)(2,1)} async-done(((bf16[16,160,256]{2,1,0:T(8,128)(2,1)}), bf16[16,160,256]{2,1,0:T(8,128)(2,1)}) %all-reduce.40.cloned.1.call-update) | async-done | bytes 1310736 | tf_op jit(solution)/shard_map/psum | solution.py:132
  (158 shorter events, 180.4 us)
Async XLA Ops:
  6.5 247.3 %all-gather.11.cloned.1.call-start = ((), (), s32[]{:S(2)}) async-start(), calls=%async_computation.13 | async-start | bytes 44564480 | tf_op jit(solution)/shard_map/all_gather | solution.py:96
  11.4 68.8 %copy-start.9 = (s32[30]{0:T(128)S(1)}, s32[30]{0:T(128)}, u32[]{:S(2)}) copy-start(s32[30]{0:T(128)} %constant.268) | copy-start | bytes 364
  11.4 78.2 %copy-start.8 = (s32[24]{0:T(128)S(1)}, s32[24]{0:T(128)}, u32[]{:S(2)}) copy-start(s32[24]{0:T(128)} %constant.270) | copy-start | bytes 292
  11.4 335.0 %all-reduce.16.cloned.1.call-start = ((), (), s32[]{:S(2)}) async-start(), calls=%async_computation | async-start | bytes 1310720 | tf_op jit(solution)/shard_map/psum | solution.py:85
  281.5 64.9 %slice-start = ((f32[31,160,256]{2,1,0:T(8,128)}), f32[8,160,256]{2,1,0:T(8,128)S(1)}, s32[]{:S(2)}) async-start(f32[31,160,256]{2,1,0:T(8,128)} %param.40), calls=%async_computation.18 | async-start | bytes 2621440 | tf_op jit(solution)/shard_map/slice | solution.py:75
  284.9 198.1 %all-gather.13.cloned.1.call-start = ((), (), s32[]{:S(2)}) async-start(), calls=%async_computation.14 | async-start | bytes 22282240 | tf_op jit(solution)/shard_map/all_gather | solution.py:96
  351.2 218.8 %all-reduce.18.cloned.1.call-start = ((), (), s32[]{:S(2)}) async-start(), calls=%async_computation.1 | async-start | bytes 655360 | tf_op jit(solution)/shard_map/psum | solution.py:85
  505.3 64.7 %slice-start.1 = ((f32[31,160,256]{2,1,0:T(8,128)}), f32[4,160,256]{2,1,0:T(8,128)S(1)}, s32[]{:S(2)}) async-start(f32[31,160,256]{2,1,0:T(8,128)} %param.40), calls=%async_computation.19 | async-start | bytes 1310720 | tf_op jit(solution)/shard_map/slice | solution.py:75
  509.6 143.6 %all-gather.15.cloned.1.call-start = ((), (), s32[]{:S(2)}) async-start(), calls=%async_computation.15 | async-start | bytes 11141120 | tf_op jit(solution)/shard_map/all_gather | solution.py:96
  573.8 159.4 %all-reduce.20.cloned.1.call-start = ((), (), s32[]{:S(2)}) async-start(), calls=%async_computation.2 | async-start | bytes 327680 | tf_op jit(solution)/shard_map/psum | solution.py:85
  675.3 116.3 %all-gather.17.cloned.1.call-start = ((), (), s32[]{:S(2)}) async-start(), calls=%async_computation.16 | async-start | bytes 5570560 | tf_op jit(solution)/shard_map/all_gather | solution.py:96
  735.4 130.7 %all-reduce.22.cloned.1.call-start = ((), (), s32[]{:S(2)}) async-start(), calls=%async_computation.3 | async-start | bytes 163840 | tf_op jit(solution)/shard_map/psum | solution.py:85
  811.5 103.6 %all-gather.19.cloned.1.call-start = ((), (), s32[]{:S(2)}) async-start(), calls=%async_computation.17 | async-start | bytes 2785280 | tf_op jit(solution)/shard_map/all_gather | solution.py:96
  868.1 105.0 %all-reduce.24.cloned.1.call-start = ((), (), s32[]{:S(2)}) async-start(), calls=%async_computation.4 | async-start | bytes 163840 | tf_op jit(solution)/shard_map/psum | solution.py:132
  919.0 142.5 %all-reduce.26.cloned.1.call-start = ((), (), s32[]{:S(2)}) async-start(), calls=%async_computation.5 | async-start | bytes 655360 | tf_op jit(solution)/shard_map/psum | solution.py:123
  977.6 143.5 %all-reduce.28.cloned.1.call-start = ((), (), s32[]{:S(2)}) async-start(), calls=%async_computation.6 | async-start | bytes 327680 | tf_op jit(solution)/shard_map/psum | solution.py:132
  1063.5 148.1 %all-reduce.30.cloned.1.call-start = ((), (), s32[]{:S(2)}) async-start(), calls=%async_computation.7 | async-start | bytes 1310720 | tf_op jit(solution)/shard_map/psum | solution.py:123
  1126.5 147.3 %all-reduce.32.cloned.1.call-start = ((), (), s32[]{:S(2)}) async-start(), calls=%async_computation.8 | async-start | bytes 655360 | tf_op jit(solution)/shard_map/psum | solution.py:132
  1213.9 161.8 %all-reduce.34.cloned.1.call-start = ((), (), s32[]{:S(2)}) async-start(), calls=%async_computation.9 | async-start | bytes 2621440 | tf_op jit(solution)/shard_map/psum | solution.py:123
  1289.0 151.2 %all-reduce.36.cloned.1.call-start = ((), (), s32[]{:S(2)}) async-start(), calls=%async_computation.10 | async-start | bytes 1310720 | tf_op jit(solution)/shard_map/psum | solution.py:132
  1379.1 166.1 %all-reduce.38.cloned.1.call-start = ((), (), s32[]{:S(2)}) async-start(), calls=%async_computation.11 | async-start | bytes 5242880 | tf_op jit(solution)/shard_map/psum | solution.py:123
  1453.3 160.1 %all-reduce.40.cloned.1.call-start = ((), (), s32[]{:S(2)}) async-start(), calls=%async_computation.12 | async-start | bytes 2621440 | tf_op jit(solution)/shard_map/psum | solution.py:132
  1550.3 64.6 %copy-start.5 = (bf16[2,160,256]{2,1,0:T(8,128)(2,1)S(1)}, bf16[2,160,256]{2,1,0:T(8,128)(2,1)}, u32[]{:S(2)}) copy-start(bf16[2,160,256]{2,1,0:T(8,128)(2,1)} %all-reduce.28.cloned.1.call-done) | copy-start | bytes 491524
  1550.3 64.6 %copy-start.6 = (bf16[1,160,256]{2,1,0:T(8,128)(2,1)S(1)}, bf16[1,160,256]{2,1,0:T(8,128)(2,1)}, u32[]{:S(2)}) copy-start(bf16[1,160,256]{2,1,0:T(8,128)(2,1)} %all-reduce.24.cloned.1.call-done) | copy-start | bytes 245764
  (6 other events, 151.6 us)
Sparse Core Ops, SparseCore 0:
  11.5 242.2 all-gather.10
  285.0 61.2 all-reduce.15
  351.3 131.6 all-gather.12
  509.7 60.2 all-reduce.17
  573.9 79.2 all-gather.14
  675.4 57.6 all-reduce.19
  735.5 56.0 all-gather.16
  811.6 54.4 all-reduce.21
  868.5 46.5 all-gather.18
  919.1 53.9 all-reduce.23
  977.7 83.6 all-reduce.25
  1063.6 57.3 all-reduce.27
  1126.6 84.8 all-reduce.29
  1214.0 59.7 all-reduce.31
  1289.1 86.5 all-reduce.33
  1379.2 60.9 all-reduce.35
  1453.4 91.7 all-reduce.37
  1550.5 62.8 all-reduce.39
